TPU v7x, 256 devices: a whole 4x4x8 slice. The times are simulated.
256 devices in a mesh: wide: 32 (over z, x), narrow: 8 (over y, core).
Axes of the slice: x: 4, y: 4, z: 8, core: 2. Of those that a mesh axis runs over, the one named last changes fastest.
Arguments:
- hidden_in: bfloat16 [64, 8192], P(None, 'wide'), may hold values from -6 to 6
- attn_gain: bfloat16 [8192], P('wide'), may hold values from 0.099609375 to 1.8984375
- qkv_weight: bfloat16 [8192, 8, 10, 128], P('wide', 'narrow'), may hold values from -2 to 2
- qkv_bias: bfloat16 [8, 10, 128], P('narrow'), may hold values from -3 to 3
- cache_keys: bfloat16 [64, 8, 4096, 128], P('wide', 'narrow'), may hold values from -256 to 256
- cache_values: bfloat16 [64, 8, 4096, 128], P('wide', 'narrow'), may hold values from -10 to 10
- positions: int32 [64, 3, 4096], P('wide'), may hold values from 0 to 4095
- lengths: int32 [64], P('wide'), may hold values from 512 to 4095, as said below
- out_weight: bfloat16 [8192, 8192], P('narrow', 'wide'), may hold values from -0.0625 to 0.0625
- mlp_gain: bfloat16 [8192], P('wide'), may hold values from 0.099609375 to 1.8984375
- gate_up_weight: bfloat16 [8192, 2, 29568], P('wide', None, 'narrow'), may hold values from -0.0625 to 0.0625
- down_weight: bfloat16 [29568, 8192], P('narrow', 'wide'), may hold values from -0.03125 to 0.03125
Outputs:
- layer_out: bfloat16 [64, 8192], P(None, 'wide')
Inputs may be any that keep to these rules, and one draw needn't show every extreme that they name: Slots 0 to lengths[b] - 1 of request b are filled, the new token takes slot lengths[b], and some request has 4095.
All inputs are finite; a program needn't handle non-finite values.
Results may differ from a plain program's by a relative error of at most 0.01115.
The roundings to bfloat16 on the way count: a program that leaves them out, or rounds other values in their place, can miss the bound.
Values may be sent and summed in bfloat16 or wider, within the bound.
No kernel may reach another device: no remote copies, remote signals or barrier semaphores. Data moves between devices by JAX's collectives and lax.ppermute only.
A program may use at most 64 MiB of HBM per device.

v0:
```python
import math
import jax
import jax.numpy as jnp
from jax import lax
from jax.sharding import PartitionSpec as P

D = 8192
DH = 128
CACHE = 4096
norm_eps = 1e-06
rope_base = 1000000.0


def mrope_tables(position):
    half_width = DH // 2
    pair_index = jnp.arange(half_width)
    inv_freq = jnp.exp(pair_index.astype(jnp.float32) * (-2.0 * math.log(rope_base) / DH))
    component = (pair_index >= DH // 8).astype(jnp.int32) + (
        pair_index >= DH // 8 + 3 * DH // 16
    ).astype(jnp.int32)
    pos_float = position.astype(jnp.float32)
    chosen = jnp.where(
        component == 0,
        pos_float[..., 0, :, None],
        jnp.where(component == 1, pos_float[..., 1, :, None], pos_float[..., 2, :, None]),
    )
    angles = chosen * inv_freq
    return (jnp.cos(angles), jnp.sin(angles))


def rotate(values, cosine, sine_table):
    half_width = values.shape[-1] // 2
    leading = values[..., :half_width]
    trailing = values[..., half_width:]
    return jnp.concatenate(
        [leading * cosine - trailing * sine_table, trailing * cosine + leading * sine_table],
        axis=-1,
    )


def local(
    hidden_in,
    attn_gain,
    qkv_weight,
    qkv_bias,
    cache_keys,
    cache_values,
    positions,
    lengths,
    out_weight,
    mlp_gain,
    gate_up_weight,
    down_weight,
):
    score_scale = 1.0 / math.sqrt(DH)
    owned = lengths.shape[0]
    local_rows = hidden_in.shape[1]
    kv_local = qkv_weight.shape[1]
    slot_count = qkv_weight.shape[2]
    group_size = slot_count - 2
    width = kv_local * slot_count * DH
    inputs = hidden_in.astype(jnp.float32)
    local_squares = jnp.sum(inputs * inputs, axis=1)
    scaled = (inputs * attn_gain.astype(jnp.float32)).astype(jnp.bfloat16)
    weight_flat = qkv_weight.reshape(local_rows, width)
    inv_rms = 1.0 / jnp.sqrt(lax.psum(local_squares, "wide") / D + norm_eps)
    row_block = scaled
    factor = inv_rms
    projected = lax.psum_scatter(
        factor[:, None] * jnp.dot(row_block, weight_flat, preferred_element_type=jnp.float32),
        "wide",
        scatter_dimension=0,
        tiled=True,
    )
    projected = projected + qkv_bias.reshape(width).astype(jnp.float32)
    projected = projected.reshape(owned, kv_local, slot_count, DH)
    cosine, sine_table = mrope_tables(positions)
    keys_rot = rotate(cache_keys.astype(jnp.float32), cosine[:, None], sine_table[:, None]).astype(
        jnp.bfloat16
    )
    new_position = jnp.take_along_axis(positions, lengths[:, None, None], axis=2)
    cos_new, sin_new = mrope_tables(new_position)
    query = rotate(projected[:, :, :group_size], cos_new[:, None], sin_new[:, None]).astype(
        jnp.bfloat16
    )
    key_new = rotate(projected[:, :, group_size], cos_new, sin_new).astype(jnp.bfloat16)
    value_new = projected[:, :, group_size + 1].astype(jnp.bfloat16)
    scores = (
        jnp.einsum("rgjd,rgsd->rgjs", query, keys_rot, preferred_element_type=jnp.float32)
        * score_scale
    )
    own_score = (
        jnp.sum(query.astype(jnp.float32) * key_new.astype(jnp.float32)[:, :, None, :], axis=3)
        * score_scale
    )
    valid_slot = jnp.arange(CACHE)[None, None, None, :] < lengths[:, None, None, None]
    row_max = jnp.maximum(jnp.max(jnp.where(valid_slot, scores, -jnp.inf), axis=3), own_score)
    probabilities = jnp.where(valid_slot, jnp.exp(scores - row_max[..., None]), 0.0)
    own_prob = jnp.exp(own_score - row_max)
    totals = jnp.sum(probabilities, axis=3) + own_prob
    probs_rounded = probabilities.astype(jnp.bfloat16)
    own_rounded = own_prob.astype(jnp.bfloat16).astype(jnp.float32)
    weighted = jnp.einsum(
        "rgjs,rgsd->rgjd", probs_rounded, cache_values, preferred_element_type=jnp.float32
    )
    weighted = weighted + own_rounded[..., None] * value_new.astype(jnp.float32)[:, :, None, :]
    attended = (
        (weighted / totals[..., None])
        .astype(jnp.bfloat16)
        .reshape(owned, kv_local * group_size * DH)
    )
    head_partial = jnp.dot(
        lax.all_gather(attended, "wide", axis=0, tiled=True),
        out_weight,
        preferred_element_type=jnp.float32,
    )
    attn_out = lax.psum(head_partial, "narrow")
    residual = (inputs + attn_out).astype(jnp.bfloat16)
    resid_float = residual.astype(jnp.float32)
    resid_squares = jnp.sum(resid_float * resid_float, axis=1)
    scaled2 = (resid_float * mlp_gain.astype(jnp.float32)).astype(jnp.bfloat16)
    hidden_local = gate_up_weight.shape[2]
    gate_up_flat = gate_up_weight.reshape(local_rows, 2 * hidden_local)
    inv_rms2 = 1.0 / jnp.sqrt(lax.psum(resid_squares, "wide") / D + norm_eps)
    row_block = scaled2
    factor = inv_rms2
    gate_up = lax.psum_scatter(
        factor[:, None] * jnp.dot(row_block, gate_up_flat, preferred_element_type=jnp.float32),
        "wide",
        scatter_dimension=0,
        tiled=True,
    )
    hidden = (jax.nn.silu(gate_up[:, :hidden_local]) * gate_up[:, hidden_local:]).astype(
        jnp.bfloat16
    )
    down_partial = jnp.dot(
        lax.all_gather(hidden, "wide", axis=0, tiled=True),
        down_weight,
        preferred_element_type=jnp.float32,
    )
    mlp_out = lax.psum(down_partial, "narrow")
    return (resid_float + mlp_out).astype(jnp.bfloat16)


def solution(mesh):
    in_specs = (
        P(None, "wide"),
        P("wide"),
        P("wide", "narrow", None, None),
        P("narrow", None, None),
        P("wide", "narrow", None, None),
        P("wide", "narrow", None, None),
        P("wide", None, None),
        P("wide"),
        P("narrow", "wide"),
        P("wide"),
        P("wide", None, "narrow"),
        P("narrow", "wide"),
    )
    out_specs = P(None, "wide")
    return jax.shard_map(local, mesh=mesh, in_specs=in_specs, out_specs=out_specs, check_vma=False)
```

profile of v0, /device:TPU:2, one launch (start us, length us, event | category | flops | bytes accessed | tf_op | source)
XLA Modules:
  0.0 691.7 jit_solution(1203411043637431055)
XLA Ops:
  6.5 1.5 copy.20
  8.0 0.9 fusion.24
  8.9 73.7 %psum.28 = f32[64]{0:T(128)S(1)} all-reduce(f32[64]{0:T(128)S(1)} %fusion.24), channel_id=1, replica_groups=mesh['wide'=32,'narrow'=8] {'wide'}, use_global_device_ids=true, to_apply=%region_1.0 | all-reduce | flops 64 | bytes 512 | tf_op jit(solution)/shard_map/psum | solution.py:66
  82.6 0.7 convert_element_type.170
  83.3 1.8 convolution_multiply_fusion.2
  85.1 0.0 all-reduce.11.cloned.1.call-update
  85.1 0.0 all-reduce.7.cloned.1.call-start
  85.2 0.9 convert_element_type.179
  86.1 3.4 copy.22
  89.6 0.1 iota_compare_fusion
  89.7 3.8 bitcast_convert_fusion
  93.5 0.1 copy.21
  93.6 0.2 or_reduce_fusion
  93.8 1.4 gather_fusion
  95.2 0.1 fusion.41
  95.3 0.2 slice_reduce_fusion.1
  95.5 0.1 fusion.51
  95.6 19.8 %fusion.7 = (bf16[2,4096,64]{2,1,0:T(8,128)(2,1)}, bf16[2,4096,64]{2,1,0:T(8,128)(2,1)}) fusion(f32[2,1,4096,128]{3,2,0,1:T(8,128)} %bitcast_convert_fusion, f32[64]{0:T(128)S(1)} %multiply_exponential_fusion, f32[2,4096]{1,0:T(2,128)S(1)} %get-tuple-element.17, f32[2,4096]{1,0:T(2,128)S(1)} %get-tuple-element.18, f32[2,4096]{1,0:T(2,128)S(1)} %get-tuple-element.16, ...), kind=kLoop, calls=%fused_computation.15 | loop fusion | flops 5767168 | bytes 6390144 | tf_op jit(solution)/shard_map/concatenate | solution.py:35
  115.4 0.1 fusion.50
  115.6 0.6 dynamic-slice
  116.8 112.9 %all-reduce.11.cloned.1.call-done = f32[64,1280]{1,0:T(8,128)} async-done(((f32[64,1280]{1,0:T(8,128)}), f32[64,1280]{1,0:T(8,128)}) %all-reduce.11.cloned.1.call-update) | async-done | bytes 327696
  229.7 0.8 dynamic-slice_add_fusion
  230.6 0.1 subtract_convert_fusion.1
  230.6 0.1 fusion.43
  230.7 0.1 maximum_convert_fusion
  230.8 0.2 multiply_reduce_fusion
  231.0 3.6 select_reduce_fusion
  234.6 0.2 fusion.18
  234.8 0.4 fusion.15
  235.3 41.5 %all-gather = bf16[32,2,1024]{2,1,0:T(2,128)(2,1)S(1)} all-gather(bf16[1,2,1024]{2,1,0:T(2,128)(2,1)S(1)} %reshape.655), channel_id=1, replica_groups=mesh['wide'=32,'narrow'=8] {'wide'}, dimensions={0}, use_global_device_ids=true | all-gather | bytes 135168 | tf_op jit(solution)/shard_map/all_gather | solution.py:113
  276.8 0.1 reshape.656
  276.9 0.8 fusion.52
  277.7 0.0 all-reduce.7.cloned.1.call-update
  277.7 0.0 all-reduce.13.cloned.1.call-start
  277.8 63.5 %all-reduce.7.cloned.1.call-done = f32[64,256]{1,0:T(8,128)} async-done(((f32[64,256]{1,0:T(8,128)}), f32[64,256]{1,0:T(8,128)}) %all-reduce.7.cloned.1.call-update) | async-done | bytes 65552 | tf_op jit(solution)/shard_map/psum | solution.py:117
  341.3 0.9 fusion.27
  342.3 71.1 %psum.30 = f32[64]{0:T(128)S(1)} all-reduce(f32[64]{0:T(128)S(1)} %get-tuple-element.8), channel_id=1, replica_groups=mesh['wide'=32,'narrow'=8] {'wide'}, use_global_device_ids=true, to_apply=%region_8.9 | all-reduce | flops 64 | bytes 512 | tf_op jit(solution)/shard_map/psum | solution.py:124
  413.4 4.6 convolution_multiply_fusion
  418.0 0.0 all-reduce.13.cloned.1.call-update
  418.0 0.0 all-reduce.9.cloned.1.call-start
  418.1 149.5 %all-reduce.13.cloned.1.call-done = f32[64,7392]{1,0:T(8,128)} async-done(((f32[64,7392]{1,0:T(8,128)}), f32[64,7392]{1,0:T(8,128)}) %all-reduce.13.cloned.1.call-update) | async-done | bytes 1892368
  567.6 1.1 fusion.36
  568.7 48.7 %all-gather.1 = bf16[32,2,3696]{2,1,0:T(2,128)(2,1)S(1)} all-gather(bf16[1,2,3696]{2,1,0:T(2,128)(2,1)S(1)} %fusion.36), channel_id=1, replica_groups=mesh['wide'=32,'narrow'=8] {'wide'}, dimensions={0}, use_global_device_ids=true | all-gather | bytes 487872 | tf_op jit(solution)/shard_map/all_gather | solution.py:137
  617.3 0.4 reshape.658
  617.7 2.6 fusion.53
  620.3 0.0 all-reduce.9.cloned.1.call-update
  620.3 63.4 %all-reduce.9.cloned.1.call-done = f32[64,256]{1,0:T(8,128)} async-done(((f32[64,256]{1,0:T(8,128)}), f32[64,256]{1,0:T(8,128)}) %all-reduce.9.cloned.1.call-update) | async-done | bytes 65552 | tf_op jit(solution)/shard_map/psum | solution.py:141
  683.7 1.5 fusion.29
  (33 shorter events, 0.2 us)
Async XLA Ops:
  6.5 228.3 %copy-start = (bf16[2,1,4096,128]{3,2,1,0:T(8,128)(2,1)S(1)}, bf16[2,1,4096,128]{3,2,1,0:T(8,128)(2,1)}, u32[]{:S(2)}) copy-start(bf16[2,1,4096,128]{3,2,1,0:T(8,128)(2,1)} %param.17) | copy-start | bytes 6291460
  6.5 83.0 %copy-start.4 = (s32[2]{0:T(128)S(1)}, s32[2]{0:T(128)}, u32[]{:S(2)}) copy-start(s32[2]{0:T(128)} %param.19) | copy-start | bytes 28
  6.5 223.2 %all-reduce.11.cloned.1.call-start = ((), (), s32[]{:S(2)}) async-start(), calls=%async_computation.2 | async-start | bytes 655360
  85.1 256.2 %all-reduce.7.cloned.1.call-start = ((), (), s32[]{:S(2)}) async-start(), calls=%async_computation | async-start | bytes 131072 | tf_op jit(solution)/shard_map/psum | solution.py:117
  95.6 20.0 %copy-start.6 = (u32[256]{0:T(256)S(1)}, u32[256]{0:T(256)}, u32[]{:S(2)}) copy-start(u32[256]{0:T(256)} %constant.61) | copy-start | bytes 3076
  95.6 21.2 %copy-start.3 = (bf16[1,10,128]{2,1,0:T(8,128)(2,1)S(1)}, bf16[1,10,128]{2,1,0:T(8,128)(2,1)}, u32[]{:S(2)}) copy-start(bf16[1,10,128]{2,1,0:T(8,128)(2,1)} %param.15) | copy-start | bytes 7684
  231.0 45.9 %copy-start.1 = (bf16[1024,256]{1,0:T(8,128)(2,1)S(1)}, bf16[1024,256]{1,0:T(8,128)(2,1)}, u32[]{:S(2)}) copy-start(bf16[1024,256]{1,0:T(8,128)(2,1)} %param.20) | copy-start | bytes 1572868
  231.0 46.8 %copy-start.5 = (bf16[256]{0:T(256)(128)(2,1)S(1)}, bf16[256]{0:T(256)(128)(2,1)}, u32[]{:S(2)}) copy-start(bf16[256]{0:T(256)(128)(2,1)} %param.21) | copy-start | bytes 1540
  231.0 110.4 %copy-start.2 = (bf16[64,256]{1,0:T(8,128)(2,1)S(1)}, bf16[64,256]{1,0:T(8,128)(2,1)}, u32[]{:S(2)}) copy-start(bf16[64,256]{1,0:T(8,128)(2,1)} %param.12) | copy-start | bytes 98308
  277.7 289.9 %all-reduce.13.cloned.1.call-start = ((), (), s32[]{:S(2)}) async-start(), calls=%async_computation.3 | async-start | bytes 3801088
  418.0 265.6 %all-reduce.9.cloned.1.call-start = ((), (), s32[]{:S(2)}) async-start(), calls=%async_computation.1 | async-start | bytes 131072 | tf_op jit(solution)/shard_map/psum | solution.py:141
Sparse Core Ops, SparseCore 0:
  85.3 144.4 all-reduce.10
  277.9 63.4 all-reduce.6
  418.2 149.3 all-reduce.12
  620.4 63.1 all-reduce.8
where the time goes:
time: 692 us
  waiting for transfers between devices  389 us (56%)
  blocking collectives  235 us (34%)
  other arithmetic  31.6 us (5%)
  between operations  14 us (2%)
  matrix products  13.9 us (2%)
  local copies, waits for them, and re-layouts  7.72 us (1%)
    unnamed x6, waiting for transfers between devices  262 us
    psum x1, blocking collectives, local(): inv_rms = 1.0 / jnp.sqrt(lax.psum(local_squares, 'wide') / D + norm_eps)  73.7 us
    psum x1, blocking collectives, local(): inv_rms2 = 1.0 / jnp.sqrt(lax.psum(resid_squares, 'wide') / D + norm_eps)  71.1 us
    psum x1, waiting for transfers between devices, local(): attn_out = lax.psum(head_partial, 'narrow')  63.5 us
    psum x1, waiting for transfers between devices, local(): mlp_out = lax.psum(down_partial, 'narrow')  63.4 us
    all_gather x1, blocking collectives, local(): lax.all_gather(hidden, 'wide', axis=0, tiled=True)  48.7 us
    all_gather x1, blocking collectives, local(): lax.all_gather(attended, 'wide', axis=0, tiled=True)  41.5 us
    concatenate x2, other arithmetic, rotate(): jnp.concatenate([leading * cosine - trailing * sine_table, trailing * cos...  19.8 us
  transfers between devices with their start and end apart: 4, of which 4 were waited for; matrix products, arithmetic and copies ran while one was open for 4% of the time, Pallas kernels for 0%

commit v1 on v0

--- a/solution.py
+++ b/solution.py
@@ -134,7 +134,15 @@
         jnp.bfloat16
     )
     down_partial = jnp.dot(
-        lax.all_gather(hidden, "wide", axis=0, tiled=True),
+        jnp.concatenate(
+            lax.all_to_all(
+                jnp.stack([hidden for _ in range(lax.axis_size("wide"))]),
+                axis_name="wide",
+                split_axis=0,
+                concat_axis=0,
+            ),
+            axis=0,
+        ),
         down_weight,
         preferred_element_type=jnp.float32,
     )

time: 692 us -> 662 us (0.957)
  blocking collectives: 235 us -> 206 us
    all_gather x1 -> x0, blocking collectives: 48.7 us -> none  [local(): lax.all_gather(hidden, 'wide', axis=0, tiled=True)]
    all_to_all x0 -> x1, blocking collectives: none -> 19.5 us  [local(): lax.all_to_all(jnp.stack([hidden for _ in range(lax.axis_size('wide'))]),...]
  transfers between devices with their start and end apart: 4 -> 4, of which waited for: 4 -> 4; matrix products, arithmetic and copies ran while one was open for 4% -> 5% of each run, Pallas kernels for 0% -> 0%
where the time goes in v1:
time: 662 us; the launch traced here: 661 us
  waiting for transfers between devices  388 us (59%)
  blocking collectives  206 us (31%)
  other arithmetic  31.6 us (5%)
  between operations  14 us (2%)
  matrix products  13.9 us (2%)
  local copies, waits for them, and re-layouts  7.97 us (1%)
    unnamed x6, waiting for transfers between devices  262 us
    psum x1, blocking collectives, local(): inv_rms = 1.0 / jnp.sqrt(lax.psum(local_squares, 'wide') / D + norm_eps)  73.7 us
    psum x1, blocking collectives, local(): inv_rms2 = 1.0 / jnp.sqrt(lax.psum(resid_squares, 'wide') / D + norm_eps)  71.1 us
    psum x1, waiting for transfers between devices, local(): attn_out = lax.psum(head_partial, 'narrow')  63.5 us
    psum x1, waiting for transfers between devices, local(): mlp_out = lax.psum(down_partial, 'narrow')  61.7 us
    all_gather x1, blocking collectives, local(): lax.all_gather(attended, 'wide', axis=0, tiled=True)  41.5 us
    concatenate x2, other arithmetic, rotate(): jnp.concatenate([leading * cosine - trailing * sine_table, trailing * cos...  19.8 us
    all_to_all x1, blocking collectives, local(): lax.all_to_all(jnp.stack([hidden for _ in range(lax.axis_size('wide'))]),...  19.5 us
  transfers between devices with their start and end apart: 4, of which 4 were waited for; matrix products, arithmetic and copies ran while one was open for 5% of the time, Pallas kernels for 0%

profile of v1, /device:TPU:2, one launch (start us, length us, event | category | flops | bytes accessed | tf_op | source)
XLA Modules:
  0.0 661.1 jit_solution(6523068267170204250)
XLA Ops:
  6.5 1.5 copy.20
  8.0 0.9 fusion.24
  8.9 73.7 %psum.28 = f32[64]{0:T(128)S(1)} all-reduce(f32[64]{0:T(128)S(1)} %fusion.24), channel_id=1, replica_groups=mesh['wide'=32,'narrow'=8] {'wide'}, use_global_device_ids=true, to_apply=%region_1.0 | all-reduce | flops 64 | bytes 512 | tf_op jit(solution)/shard_map/psum | solution.py:66
  82.6 0.7 convert_element_type.170
  83.3 1.8 convolution_multiply_fusion.2
  85.1 0.0 all-reduce.11.cloned.1.call-update
  85.1 0.0 all-reduce.7.cloned.1.call-start
  85.2 0.9 convert_element_type.179
  86.1 3.4 copy.22
  89.6 0.1 iota_compare_fusion
  89.7 3.8 bitcast_convert_fusion
  93.5 0.1 copy.21
  93.6 0.2 or_reduce_fusion
  93.8 1.4 gather_fusion
  95.2 0.1 fusion.40
  95.3 0.2 slice_reduce_fusion.1
  95.5 0.1 fusion.50
  95.6 19.8 %fusion.7 = (bf16[2,4096,64]{2,1,0:T(8,128)(2,1)}, bf16[2,4096,64]{2,1,0:T(8,128)(2,1)}) fusion(f32[2,1,4096,128]{3,2,0,1:T(8,128)} %bitcast_convert_fusion, f32[64]{0:T(128)S(1)} %multiply_exponential_fusion, f32[2,4096]{1,0:T(2,128)S(1)} %get-tuple-element.17, f32[2,4096]{1,0:T(2,128)S(1)} %get-tuple-element.18, f32[2,4096]{1,0:T(2,128)S(1)} %get-tuple-element.16, ...), kind=kLoop, calls=%fused_computation.15 | loop fusion | flops 5767168 | bytes 6390144 | tf_op jit(solution)/shard_map/concatenate | solution.py:35
  115.4 0.1 fusion.49
  115.6 0.6 dynamic-slice
  116.8 112.9 %all-reduce.11.cloned.1.call-done = f32[64,1280]{1,0:T(8,128)} async-done(((f32[64,1280]{1,0:T(8,128)}), f32[64,1280]{1,0:T(8,128)}) %all-reduce.11.cloned.1.call-update) | async-done | bytes 327696
  229.7 0.8 dynamic-slice_add_fusion
  230.6 0.1 subtract_convert_fusion.1
  230.6 0.1 fusion.42
  230.7 0.1 maximum_convert_fusion
  230.8 0.2 multiply_reduce_fusion
  231.0 3.6 select_reduce_fusion
  234.6 0.2 fusion.18
  234.8 0.4 fusion.15
  235.3 41.5 %all-gather = bf16[32,2,1024]{2,1,0:T(2,128)(2,1)S(1)} all-gather(bf16[1,2,1024]{2,1,0:T(2,128)(2,1)S(1)} %reshape.661), channel_id=1, replica_groups=mesh['wide'=32,'narrow'=8] {'wide'}, dimensions={0}, use_global_device_ids=true | all-gather | bytes 135168 | tf_op jit(solution)/shard_map/all_gather | solution.py:113
  276.8 0.1 reshape.662
  276.9 0.8 fusion.51
  277.7 0.0 all-reduce.7.cloned.1.call-update
  277.7 0.0 all-reduce.13.cloned.1.call-start
  277.8 63.5 %all-reduce.7.cloned.1.call-done = f32[64,256]{1,0:T(8,128)} async-done(((f32[64,256]{1,0:T(8,128)}), f32[64,256]{1,0:T(8,128)}) %all-reduce.7.cloned.1.call-update) | async-done | bytes 65552 | tf_op jit(solution)/shard_map/psum | solution.py:117
  341.3 0.9 fusion.27
  342.3 71.1 %psum.30 = f32[64]{0:T(128)S(1)} all-reduce(f32[64]{0:T(128)S(1)} %get-tuple-element.8), channel_id=1, replica_groups=mesh['wide'=32,'narrow'=8] {'wide'}, use_global_device_ids=true, to_apply=%region_8.9 | all-reduce | flops 64 | bytes 512 | tf_op jit(solution)/shard_map/psum | solution.py:124
  413.4 4.6 convolution_multiply_fusion
  418.0 0.0 all-reduce.13.cloned.1.call-update
  418.0 0.0 all-reduce.9.cloned.1.call-start
  418.1 149.5 %all-reduce.13.cloned.1.call-done = f32[64,7392]{1,0:T(8,128)} async-done(((f32[64,7392]{1,0:T(8,128)}), f32[64,7392]{1,0:T(8,128)}) %all-reduce.13.cloned.1.call-update) | async-done | bytes 1892368
  567.6 1.1 fusion.35
  568.7 0.2 stack.2
  568.9 19.5 %all_to_all.5 = bf16[32,2,3696]{2,1,0:T(2,128)(2,1)S(1)} all-to-all(bf16[32,2,3696]{2,1,0:T(2,128)(2,1)S(1)} %stack.2), channel_id=1, replica_groups=mesh['wide'=32,'narrow'=8] {'wide'}, dimensions={0} | all-to-all | bytes 946176 | tf_op jit(solution)/shard_map/all_to_all | solution.py:138
  588.4 0.4 reshape.650
  588.8 2.6 fusion.52
  591.4 61.7 %all-reduce.9.cloned.1.call-done = f32[64,256]{1,0:T(8,128)} async-done(((f32[64,256]{1,0:T(8,128)}), f32[64,256]{1,0:T(8,128)}) %all-reduce.9.cloned.1.call-update) | async-done | bytes 65552 | tf_op jit(solution)/shard_map/psum | solution.py:149
  653.1 1.5 fusion.29
  (34 shorter events, 0.2 us)
Async XLA Ops:
  6.5 228.3 %copy-start = (bf16[2,1,4096,128]{3,2,1,0:T(8,128)(2,1)S(1)}, bf16[2,1,4096,128]{3,2,1,0:T(8,128)(2,1)}, u32[]{:S(2)}) copy-start(bf16[2,1,4096,128]{3,2,1,0:T(8,128)(2,1)} %param.17) | copy-start | bytes 6291460
  6.5 83.0 %copy-start.4 = (s32[2]{0:T(128)S(1)}, s32[2]{0:T(128)}, u32[]{:S(2)}) copy-start(s32[2]{0:T(128)} %param.19) | copy-start | bytes 28
  6.5 223.2 %all-reduce.11.cloned.1.call-start = ((), (), s32[]{:S(2)}) async-start(), calls=%async_computation.3 | async-start | bytes 655360
  85.1 256.2 %all-reduce.7.cloned.1.call-start = ((), (), s32[]{:S(2)}) async-start(), calls=%async_computation.1 | async-start | bytes 131072 | tf_op jit(solution)/shard_map/psum | solution.py:117
  95.6 20.0 %copy-start.6 = (u32[256]{0:T(256)S(1)}, u32[256]{0:T(256)}, u32[]{:S(2)}) copy-start(u32[256]{0:T(256)} %constant.61) | copy-start | bytes 3076
  95.6 21.2 %copy-start.3 = (bf16[1,10,128]{2,1,0:T(8,128)(2,1)S(1)}, bf16[1,10,128]{2,1,0:T(8,128)(2,1)}, u32[]{:S(2)}) copy-start(bf16[1,10,128]{2,1,0:T(8,128)(2,1)} %param.15) | copy-start | bytes 7684
  231.0 45.9 %copy-start.1 = (bf16[1024,256]{1,0:T(8,128)(2,1)S(1)}, bf16[1024,256]{1,0:T(8,128)(2,1)}, u32[]{:S(2)}) copy-start(bf16[1024,256]{1,0:T(8,128)(2,1)} %param.20) | copy-start | bytes 1572868
  231.0 46.8 %copy-start.5 = (bf16[256]{0:T(256)(128)(2,1)S(1)}, bf16[256]{0:T(256)(128)(2,1)}, u32[]{:S(2)}) copy-start(bf16[256]{0:T(256)(128)(2,1)} %param.21) | copy-start | bytes 1540
  231.0 110.4 %copy-start.2 = (bf16[64,256]{1,0:T(8,128)(2,1)S(1)}, bf16[64,256]{1,0:T(8,128)(2,1)}, u32[]{:S(2)}) copy-start(bf16[64,256]{1,0:T(8,128)(2,1)} %param.12) | copy-start | bytes 98308
  277.7 289.9 %all-reduce.13.cloned.1.call-start = ((), (), s32[]{:S(2)}) async-start(), calls=%async_computation.4 | async-start | bytes 3801088
  418.0 235.1 %all-reduce.9.cloned.1.call-start = ((), (), s32[]{:S(2)}) async-start(), calls=%async_computation.2 | async-start | bytes 131072 | tf_op jit(solution)/shard_map/psum | solution.py:149
Sparse Core Ops, SparseCore 0:
  85.3 144.4 all-reduce.10
  277.9 63.4 all-reduce.6
  418.2 149.3 all-reduce.12
  591.5 61.5 all-reduce.8
